TPU v7x, 128 devices: a whole 4x4x4 slice. The times are simulated.
128 devices in a mesh: epoch: 8 (over z, y_hi), row: 16 (over y_lo, x, core).
Axes of the slice: x: 4, y: 4 (y_hi: 2, y_lo: 2; y = y_hi * 2 + y_lo), z: 4, core: 2. Of those that a mesh axis runs over, the one named last changes fastest.
Arguments:
- field: bfloat16 [1024, 512, 512], P('epoch', 'row'), may hold values from -6 to 6
- factor: bfloat16 [1024, 1024], P('epoch'), may hold values from -0.1875 to 0.1875
- kappa: float32 [512, 512], P('row'), may hold values from 0.05 to 1
Outputs:
- product: float32 [1024, 512, 512], P('epoch', 'row')
All inputs are finite; a program needn't handle non-finite values.
Results may differ from a plain program's by a relative error of at most 0.0004.
Values may be sent and summed in bfloat16 or wider, within the bound.
No kernel may reach another device: no remote copies, remote signals or barrier semaphores. Data moves between devices by JAX's collectives and lax.ppermute only.
A program may use at most 192 MiB of HBM per device.

v0:
```python
import jax
import jax.numpy as jnp
from jax import lax
from jax.sharding import PartitionSpec as P


def with_halo(x, sides, width):
    for axis, dim in sides:
        size, length = (lax.axis_size(axis), x.shape[dim])
        up = [(i, (i + 1) % size) for i in range(size - 1)]
        down = [(j, i) for i, j in up]
        last = lax.slice_in_dim(x, length - width, length, axis=dim)
        first = lax.slice_in_dim(x, 0, width, axis=dim)
        before = lax.ppermute(last, axis, up)
        after = lax.ppermute(first, axis, down)
        x = jnp.concatenate([before, x, after], axis=dim)
    return x


def stencil(padded, kappa):
    center = padded[:, 1:-1, :]
    sides = jnp.pad(center, ((0, 0), (0, 0), (1, 1)))
    upper = padded[:, :-2, :]
    below = padded[:, 2:, :]
    return (kappa + 4.0) * center - (upper + below + sides[:, :, :-2] + sides[:, :, 2:])


def single_rim(values):
    return with_halo(values, (("row", 1),), 1)


def body(field, factor, kappa):
    epochs = field.shape[0]
    slab = field.shape[1]
    width = field.shape[2]
    count = lax.axis_size("epoch")
    order = epochs * count
    global_rows = lax.axis_index("epoch") * epochs + lax.broadcasted_iota(
        jnp.int32, (epochs, order), 0
    )
    global_cols = lax.broadcasted_iota(jnp.int32, (epochs, order), 1)
    lower = jnp.where(global_cols <= global_rows, factor, jnp.zeros_like(factor))
    piece = lax.all_gather(field, "epoch", axis=0, tiled=True)
    many = piece.shape[0]
    timed = jnp.dot(
        lower, piece.reshape(many, slab * width), preferred_element_type=jnp.float32
    ).reshape(epochs, slab, width)
    first = stencil(single_rim(timed), kappa)
    return stencil(single_rim(first), kappa)


def solution(mesh):
    in_specs = (P("epoch", "row", None), P("epoch", None), P("row", None))
    out_specs = P("epoch", "row", None)
    return jax.shard_map(body, mesh=mesh, in_specs=in_specs, out_specs=out_specs, check_vma=False)
```

profile of v0, /device:TPU:7, one launch (start us, length us, event | category | flops | bytes accessed | tf_op | source)
XLA Modules:
  0.0 493.1 jit_solution(14374441201835860905)
XLA Ops:
  6.5 0.0 all-gather.2.cloned.1.call-start
  6.5 0.7 all-gather.2.cloned.1.call-update
  7.3 0.0 copy-start
  7.3 338.7 %all-gather.2.cloned.1.call-done = bf16[1024,32,512]{2,1,0:T(8,128)(2,1)} async-done(((bf16[128,32,512]{2,1,0:T(8,128)(2,1)}), bf16[1024,32,512]{2,1,0:T(8,128)(2,1)}) %all-gather.2.cloned.1.call-update) | async-done | bytes 33554448 | tf_op jit(solution)/shard_map/all_gather | solution.py:43
  345.9 45.1 %copy.8 = bf16[1024,32,512]{0,2,1:T(8,128)(2,1)} copy(bf16[1024,32,512]{2,1,0:T(8,128)(2,1)} %all-gather.2.cloned.1.call-done) | data formatting | bytes 67108864 | tf_op jit(solution)/shard_map/reshape | solution.py:46
  391.1 0.0 copy-done
  391.1 0.0 copy-start.1
  391.1 18.8 %fusion = f32[128,32,512]{2,0,1:T(8,128)} fusion(bf16[1024,32,512]{0,2,1:T(8,128)(2,1)} %copy.8, bf16[128,1024]{1,0:T(8,128)(2,1)S(1)} %copy-done, s32[128]{0:T(128)S(1)} %iota_add_fusion), kind=kOutput, calls=%fused_computation | convolution fusion | flops 4295229440 | bytes 42205696 | tf_op jit(solution)/shard_map/dot_general | solution.py:45
  409.9 1.1 fusion.17
  411.0 3.2 collective-permute-start
  414.1 1.9 collective-permute-start.1
  416.1 0.0 copy-done.1
  416.1 1.3 collective-permute-done
  417.4 6.5 %collective-permute-done.1 = f32[128,1,512]{2,0,1:T(8,128)S(1)} collective-permute-done((f32[128,1,512]{2,0,1:T(8,128)S(1)}, f32[128,1,512]{2,0,1:T(8,128)S(1)}, u32[]{:S(2)}, u32[]{:S(2)}) %collective-permute-start.1) | collective-permute-done | bytes 262176 | tf_op jit(solution)/shard_map/ppermute | solution.py:15
  423.9 18.9 %fusion.4 = f32[128,32,512]{2,0,1:T(8,128)} fusion(f32[128,32,512]{2,0,1:T(8,128)} %fusion, f32[128,1,512]{2,0,1:T(8,128)S(1)} %collective-permute-done.1, f32[128,1,512]{2,0,1:T(8,128)S(1)} %collective-permute-done, f32[32,512]{1,0:T(8,128)S(1)} %broadcast_add_fusion), kind=kLoop, calls=%fused_computation.8 | loop fusion | flops 14680064 | bytes 17367040 | tf_op jit(solution)/shard_map/sub | solution.py:25
  442.9 1.1 fusion.16
  443.9 1.9 collective-permute-start.2
  445.9 2.6 collective-permute-start.3
  448.5 0.7 collective-permute-done.2
  449.2 6.5 %collective-permute-done.3 = f32[128,1,512]{2,0,1:T(8,128)S(1)} collective-permute-done((f32[128,1,512]{2,0,1:T(8,128)S(1)}, f32[128,1,512]{2,0,1:T(8,128)S(1)}, u32[]{:S(2)}, u32[]{:S(2)}) %collective-permute-start.3) | collective-permute-done | bytes 262176 | tf_op jit(solution)/shard_map/ppermute | solution.py:15
  455.7 18.9 %fusion.7 = f32[128,32,512]{2,0,1:T(8,128)} fusion(f32[128,32,512]{2,0,1:T(8,128)} %fusion.4, f32[128,1,512]{2,0,1:T(8,128)S(1)} %collective-permute-done.3, f32[128,1,512]{2,0,1:T(8,128)S(1)} %collective-permute-done.2, f32[32,512]{1,0:T(8,128)S(1)} %broadcast_add_fusion), kind=kLoop, calls=%fused_computation.11 | loop fusion | flops 14680064 | bytes 17367040 | tf_op jit(solution)/shard_map/sub | solution.py:25
  474.6 11.6 %copy.7 = f32[128,32,512]{2,1,0:T(8,128)} copy(f32[128,32,512]{2,0,1:T(8,128)} %fusion.7) | data formatting | bytes 16777216 | tf_op jit(solution)/shard_map/sub | solution.py:25
  (2 shorter events, 0.0 us)
Async XLA Ops:
  6.5 339.4 %all-gather.2.cloned.1.call-start = ((), (), s32[]{:S(2)}) async-start(), calls=%async_computation | async-start | bytes 37748736 | tf_op jit(solution)/shard_map/all_gather | solution.py:43
  7.3 383.8 %copy-start = (bf16[128,1024]{1,0:T(8,128)(2,1)S(1)}, bf16[128,1024]{1,0:T(8,128)(2,1)}, u32[]{:S(2)}) copy-start(bf16[128,1024]{1,0:T(8,128)(2,1)} %param.4) | copy-start | bytes 786436
  391.1 25.0 %copy-start.1 = (f32[32,512]{1,0:T(8,128)S(1)}, f32[32,512]{1,0:T(8,128)}, u32[]{:S(2)}) copy-start(f32[32,512]{1,0:T(8,128)} %param.5) | copy-start | bytes 196612
  411.0 6.5 %collective-permute-start = (f32[128,1,512]{2,0,1:T(8,128)S(1)}, f32[128,1,512]{2,0,1:T(8,128)S(1)}, u32[]{:S(2)}, u32[]{:S(2)}) collective-permute-start(f32[128,1,512]{2,0,1:T(8,128)S(1)} %get-tuple-element.7), channel_id=1, source_target_pairs={{0,1},{1,2},{2,3},{3,4},{4,5},{5,6},{6,7},{7,8},{8,9},{9,10},{10,1... | collective-permute-start | bytes 786440 | tf_op jit(solution)/shard_map/ppermute | solution.py:14
  414.1 9.8 %collective-permute-start.1 = (f32[128,1,512]{2,0,1:T(8,128)S(1)}, f32[128,1,512]{2,0,1:T(8,128)S(1)}, u32[]{:S(2)}, u32[]{:S(2)}) collective-permute-start(f32[128,1,512]{2,0,1:T(8,128)S(1)} %get-tuple-element.8), channel_id=1, source_target_pairs={{1,0},{2,1},{3,2},{4,3},{5,4},{6,5},{7,6},{8,7},{9,8},{10,9},{11,1... | collective-permute-start | bytes 786440 | tf_op jit(solution)/shard_map/ppermute | solution.py:15
  443.9 5.2 %collective-permute-start.2 = (f32[128,1,512]{2,0,1:T(8,128)S(1)}, f32[128,1,512]{2,0,1:T(8,128)S(1)}, u32[]{:S(2)}, u32[]{:S(2)}) collective-permute-start(f32[128,1,512]{2,0,1:T(8,128)S(1)} %get-tuple-element.5), channel_id=1, source_target_pairs={{0,1},{1,2},{2,3},{3,4},{4,5},{5,6},{6,7},{7,8},{8,9},{9,10},{10,1... | collective-permute-start | bytes 786440 | tf_op jit(solution)/shard_map/ppermute | solution.py:14
  445.9 9.8 %collective-permute-start.3 = (f32[128,1,512]{2,0,1:T(8,128)S(1)}, f32[128,1,512]{2,0,1:T(8,128)S(1)}, u32[]{:S(2)}, u32[]{:S(2)}) collective-permute-start(f32[128,1,512]{2,0,1:T(8,128)S(1)} %get-tuple-element.6), channel_id=1, source_target_pairs={{1,0},{2,1},{3,2},{4,3},{5,4},{6,5},{7,6},{8,7},{9,8},{10,9},{11,1... | collective-permute-start | bytes 786440 | tf_op jit(solution)/shard_map/ppermute | solution.py:15
Sparse Core Ops, SparseCore 0:
  9.7 336.1 all-gather.1
where the time goes:
time: 495 us; the launch traced here: 493 us
  waiting for transfers between devices  354 us (72%)
  local copies, waits for them, and re-layouts  58.9 us (12%)
  other arithmetic  37.9 us (8%)
  matrix products  18.8 us (4%)
  between operations  13.5 us (3%)
  starting transfers between devices  9.59 us (2%)
    all_gather x1, waiting for transfers between devices, body(): piece = lax.all_gather(field, 'epoch', axis=0, tiled=True)  339 us
    reshape x1, local copies, waits for them, and re-layouts, body(): piece.reshape(many, slab * width)  45.1 us
    sub x2, other arithmetic, stencil(): (kappa + 4.0) * center  37.9 us
    dot_general x1, matrix products, body(): jnp.dot(lower, piece.reshape(many, slab * width), preferred_element_type=...  18.8 us
    ppermute x2, waiting for transfers between devices, with_halo(): after = lax.ppermute(first, axis, down)  13 us
    sub x1, local copies, waits for them, and re-layouts, stencil(): (kappa + 4.0) * center  11.6 us
  transfers between devices with their start and end apart: 5, of which 5 were waited for; matrix products, arithmetic and copies ran while one was open for 0% of the time, Pallas kernels for 0%

commit v1 on v0

--- a/solution.py
+++ b/solution.py
@@ -40,7 +40,8 @@
     )
     global_cols = lax.broadcasted_iota(jnp.int32, (epochs, order), 1)
     lower = jnp.where(global_cols <= global_rows, factor, jnp.zeros_like(factor))
-    piece = lax.all_gather(field, "epoch", axis=0, tiled=True)
+    sent = jnp.stack([field] * lax.axis_size("epoch"))
+    piece = jnp.concatenate(lax.all_to_all(sent, "epoch", 0, 0), axis=0)
     many = piece.shape[0]
     timed = jnp.dot(
         lower, piece.reshape(many, slab * width), preferred_element_type=jnp.float32

time: 495 us -> 612 us (1.24)
  local copies, waits for them, and re-layouts: 58.9 us -> 154 us
  waiting for transfers between devices: 354 us -> 381 us
  between operations: 13.5 us -> 0.07 us
  starting transfers between devices: 9.59 us -> 17.5 us
    all_to_all x0 -> x1, waiting for transfers between devices: none -> 366 us  [body(): piece = jnp.concatenate(lax.all_to_all(sent, 'epoch', 0, 0), axis=0)]
    all_gather x1 -> x0, waiting for transfers between devices: 339 us -> none  [body(): piece = lax.all_gather(field, 'epoch', axis=0, tiled=True)]
    reshape x1 -> x0, local copies, waits for them, and re-layouts: 45.1 us -> none  [body(): piece.reshape(many, slab * width)]
    all_to_all x0 -> x1, local copies, waits for them, and re-layouts: none -> 45 us  [body(): piece = jnp.concatenate(lax.all_to_all(sent, 'epoch', 0, 0), axis=0)]
    dot_general x0 -> x1, local copies, waits for them, and re-layouts: none -> 44.1 us  [body(): jnp.dot(lower, piece.reshape(many, slab * width), preferred_element_type=...]
    unnamed x4 -> x6, local copies, waits for them, and re-layouts: 0.01 us -> 38.8 us
    another operation x0 -> x1, local copies, waits for them, and re-layouts: none -> 12.6 us  [body(): sent = jnp.stack([field] * lax.axis_size('epoch'))]
    all_to_all x0 -> x1, starting transfers between devices: none -> 7.66 us  [body(): piece = jnp.concatenate(lax.all_to_all(sent, 'epoch', 0, 0), axis=0)]
where the time goes in v1:
time: 612 us; the launch traced here: 609 us
  waiting for transfers between devices  381 us (62%)
  local copies, waits for them, and re-layouts  154 us (25%)
  other arithmetic  37.7 us (6%)
  matrix products  18.8 us (3%)
  starting transfers between devices  17.5 us (3%)
    all_to_all x1, waiting for transfers between devices, body(): piece = jnp.concatenate(lax.all_to_all(sent, 'epoch', 0, 0), axis=0)  366 us
    all_to_all x1, local copies, waits for them, and re-layouts, body(): piece = jnp.concatenate(lax.all_to_all(sent, 'epoch', 0, 0), axis=0)  45 us
    dot_general x1, local copies, waits for them, and re-layouts, body(): jnp.dot(lower, piece.reshape(many, slab * width), preferred_element_type=...  44.1 us
    unnamed x6, local copies, waits for them, and re-layouts  38.8 us
    sub x2, other arithmetic, stencil(): (kappa + 4.0) * center  37.7 us
    dot_general x1, matrix products, body(): jnp.dot(lower, piece.reshape(many, slab * width), preferred_element_type=...  18.8 us
    ppermute x2, waiting for transfers between devices, with_halo(): after = lax.ppermute(first, axis, down)  13 us
    another operation x1, local copies, waits for them, and re-layouts, body(): sent = jnp.stack([field] * lax.axis_size('epoch'))  12.6 us
  transfers between devices with their start and end apart: 5, of which 5 were waited for; matrix products, arithmetic and copies ran while one was open for 0% of the time, Pallas kernels for 0%

profile of v1, /device:TPU:7, one launch (start us, length us, event | category | flops | bytes accessed | tf_op | source)
XLA Modules:
  0.0 609.4 jit_solution(6287054470292029109)
XLA Ops:
  0.0 7.9 %copy.8 = bf16[128,32,512]{0,2,1:T(8,128)(2,1)} copy(bf16[128,32,512]{2,1,0:T(8,128)(2,1)} %param.3) | data formatting | bytes 8388608 | tf_op args[0]
  7.9 12.6 %stack.2 = bf16[8,128,32,512]{1,3,2,0:T(8,128)(2,1)} broadcast(bf16[128,32,512]{0,2,1:T(8,128)(2,1)} %copy.8), dimensions={1,2,3} | broadcast | bytes 37748736 | tf_op jit(solution)/shard_map/stack | solution.py:43
  20.4 7.7 %all-to-all-start = ((bf16[8,128,32,512]{1,3,2,0:T(8,128)(2,1)}), bf16[8,128,32,512]{1,3,2,0:T(8,128)(2,1)}, u32[]{:S(2)}, u32[]{:S(2)}) async-start(bf16[8,128,32,512]{1,3,2,0:T(8,128)(2,1)} %stack.2), calls=%async_computation | async-start | bytes 67108864 | tf_op jit(solution)/shard_map/all_to_all | solution.py:44
  28.1 366.1 %all-to-all-done = bf16[8,128,32,512]{1,3,2,0:T(8,128)(2,1)} async-done(((bf16[8,128,32,512]{1,3,2,0:T(8,128)(2,1)}), bf16[8,128,32,512]{1,3,2,0:T(8,128)(2,1)}, u32[]{:S(2)}, u32[]{:S(2)}) %all-to-all-start) | async-done | bytes 33554464 | tf_op jit(solution)/shard_map/all_to_all | solution.py:44
  394.2 45.0 %copy.9 = bf16[8,128,32,512]{3,2,1,0:T(8,128)(2,1)} copy(bf16[8,128,32,512]{1,3,2,0:T(8,128)(2,1)} %all-to-all-done) | data formatting | bytes 67108864 | tf_op jit(solution)/shard_map/all_to_all | solution.py:44
  439.2 30.9 %copy.12 = bf16[128,8,32,512]{3,1,2,0:T(8,128)(2,1)} copy(bf16[128,8,32,512]{3,2,1,0:T(8,128)(2,1)} %bitcast.11) | data formatting | bytes 67108864
  470.1 0.0 copy-start
  470.1 44.1 %copy.10 = bf16[16384,1024]{1,0:T(8,128)(2,1)} copy(bf16[16384,1024]{0,1:T(8,128)(2,1)} %bitcast.12) | data formatting | bytes 67108864 | tf_op jit(solution)/shard_map/dot_general | solution.py:46
  514.2 0.0 copy-done
  514.2 18.8 %fusion.10 = f32[128,32,512]{2,0,1:T(8,128)} fusion(bf16[32,512,1024]{2,1,0:T(8,128)(2,1)} %bitcast.10, bf16[128,1024]{1,0:T(8,128)(2,1)S(1)} %copy-done, s32[128]{0:T(128)S(1)} %iota_add_fusion), kind=kOutput, calls=%fused_computation.19 | convolution fusion | flops 4295229440 | bytes 42205696 | tf_op jit(solution)/shard_map/dot_general | solution.py:46
  533.1 1.1 fusion.16
  534.1 3.4 collective-permute-start
  537.5 1.9 collective-permute-start.1
  539.4 0.0 copy-done.1
  539.4 1.3 collective-permute-done
  540.8 6.5 %collective-permute-done.1 = f32[128,1,512]{2,0,1:T(8,128)S(1)} collective-permute-done((f32[128,1,512]{2,0,1:T(8,128)S(1)}, f32[128,1,512]{2,0,1:T(8,128)S(1)}, u32[]{:S(2)}, u32[]{:S(2)}) %collective-permute-start.1) | collective-permute-done | bytes 262176 | tf_op jit(solution)/shard_map/ppermute | solution.py:15
  547.3 18.8 %fusion.2 = f32[128,32,512]{2,0,1:T(8,128)} fusion(f32[128,32,512]{2,0,1:T(8,128)} %fusion.10, f32[128,1,512]{2,0,1:T(8,128)S(1)} %collective-permute-done.1, f32[128,1,512]{2,0,1:T(8,128)S(1)} %collective-permute-done, f32[32,512]{1,0:T(8,128)S(1)} %broadcast_add_fusion), kind=kLoop, calls=%fused_computation.6 | loop fusion | flops 14680064 | bytes 17367040 | tf_op jit(solution)/shard_map/sub | solution.py:25
  566.1 1.1 fusion.15
  567.2 1.9 collective-permute-start.2
  569.1 2.6 collective-permute-start.3
  571.7 0.7 collective-permute-done.2
  572.4 6.5 %collective-permute-done.3 = f32[128,1,512]{2,0,1:T(8,128)S(1)} collective-permute-done((f32[128,1,512]{2,0,1:T(8,128)S(1)}, f32[128,1,512]{2,0,1:T(8,128)S(1)}, u32[]{:S(2)}, u32[]{:S(2)}) %collective-permute-start.3) | collective-permute-done | bytes 262176 | tf_op jit(solution)/shard_map/ppermute | solution.py:15
  578.9 18.9 %fusion.5 = f32[128,32,512]{2,0,1:T(8,128)} fusion(f32[128,32,512]{2,0,1:T(8,128)} %fusion.2, f32[128,1,512]{2,0,1:T(8,128)S(1)} %collective-permute-done.3, f32[128,1,512]{2,0,1:T(8,128)S(1)} %collective-permute-done.2, f32[32,512]{1,0:T(8,128)S(1)} %broadcast_add_fusion), kind=kLoop, calls=%fused_computation.9 | loop fusion | flops 14680064 | bytes 17367040 | tf_op jit(solution)/shard_map/sub | solution.py:25
  597.8 11.6 %copy.11 = f32[128,32,512]{2,1,0:T(8,128)} copy(f32[128,32,512]{2,0,1:T(8,128)} %fusion.5) | data formatting | bytes 16777216 | tf_op jit(solution)/shard_map/sub | solution.py:25
  (3 shorter events, 0.0 us)
Async XLA Ops:
  20.4 373.8 %all-to-all-start = ((bf16[8,128,32,512]{1,3,2,0:T(8,128)(2,1)}), bf16[8,128,32,512]{1,3,2,0:T(8,128)(2,1)}, u32[]{:S(2)}, u32[]{:S(2)}) async-start(bf16[8,128,32,512]{1,3,2,0:T(8,128)(2,1)} %stack.2), calls=%async_computation | async-start | bytes 67108864 | tf_op jit(solution)/shard_map/all_to_all | solution.py:44
  470.1 44.1 %copy-start = (bf16[128,1024]{1,0:T(8,128)(2,1)S(1)}, bf16[128,1024]{1,0:T(8,128)(2,1)}, u32[]{:S(2)}) copy-start(bf16[128,1024]{1,0:T(8,128)(2,1)} %param.4) | copy-start | bytes 786436
  514.2 25.2 %copy-start.1 = (f32[32,512]{1,0:T(8,128)S(1)}, f32[32,512]{1,0:T(8,128)}, u32[]{:S(2)}) copy-start(f32[32,512]{1,0:T(8,128)} %param.5) | copy-start | bytes 196612
  534.1 6.7 %collective-permute-start = (f32[128,1,512]{2,0,1:T(8,128)S(1)}, f32[128,1,512]{2,0,1:T(8,128)S(1)}, u32[]{:S(2)}, u32[]{:S(2)}) collective-permute-start(f32[128,1,512]{2,0,1:T(8,128)S(1)} %get-tuple-element.7), channel_id=1, source_target_pairs={{0,1},{1,2},{2,3},{3,4},{4,5},{5,6},{6,7},{7,8},{8,9},{9,10},{10,1... | collective-permute-start | bytes 786440 | tf_op jit(solution)/shard_map/ppermute | solution.py:14
  537.5 9.8 %collective-permute-start.1 = (f32[128,1,512]{2,0,1:T(8,128)S(1)}, f32[128,1,512]{2,0,1:T(8,128)S(1)}, u32[]{:S(2)}, u32[]{:S(2)}) collective-permute-start(f32[128,1,512]{2,0,1:T(8,128)S(1)} %get-tuple-element.8), channel_id=1, source_target_pairs={{1,0},{2,1},{3,2},{4,3},{5,4},{6,5},{7,6},{8,7},{9,8},{10,9},{11,1... | collective-permute-start | bytes 786440 | tf_op jit(solution)/shard_map/ppermute | solution.py:15
  567.2 5.2 collective-permute-start.2
  569.1 9.8 %collective-permute-start.3 = (f32[128,1,512]{2,0,1:T(8,128)S(1)}, f32[128,1,512]{2,0,1:T(8,128)S(1)}, u32[]{:S(2)}, u32[]{:S(2)}) collective-permute-start(f32[128,1,512]{2,0,1:T(8,128)S(1)} %get-tuple-element.6), channel_id=1, source_target_pairs={{1,0},{2,1},{3,2},{4,3},{5,4},{6,5},{7,6},{8,7},{9,8},{10,9},{11,1... | collective-permute-start | bytes 786440 | tf_op jit(solution)/shard_map/ppermute | solution.py:15
